TPU v7x, 128 devices: a whole 4x4x4 slice. The times are simulated.
128 devices in a mesh: blk: 32 (over x, z_hi, y), rep: 4 (over z_lo, core).
Axes of the slice: x: 4, y: 4, z: 4 (z_hi: 2, z_lo: 2; z = z_hi * 2 + z_lo), core: 2. Of those that a mesh axis runs over, the one named last changes fastest.
Arguments:
- queries: bfloat16 [32768, 4096], P(('blk', 'rep')), as said below
- query_group: int32 [32768, 1], P(('blk', 'rep')), may hold values from 0 to 3; in each aligned block of 256 rows (0 to 255, 256 to 511, ...) at most 128 rows name the same one
- query_bin: int32 [32768], P(('blk', 'rep')), may hold values from 0 to 63
- query_shift: int32 [32768], P(('blk', 'rep')), may hold values from 1 to 2
- library: bfloat16 [4, 1024, 4096], P('rep', 'blk'), as said below
- library_bin: int32 [4, 1024], P('rep', 'blk'), may hold values from 0 to 63
Outputs:
- best_scores: float32 [32768, 8], P(('blk', 'rep'))
Inputs may be any that keep to these rules, and one draw needn't show every extreme that they name: `query_group`: among the 256 queries of one device at most 128 name the same group, and on every draw some device has a group named by exactly 128 of its queries. `queries`: intensities are nonnegative and every spectrum has peaks. `library`: intensities are nonnegative and every spectrum has peaks.
All inputs are finite; a program needn't handle non-finite values.
Results may differ from a plain program's by a relative error of at most 0.0021.
Values may be sent and summed in bfloat16 or wider, within the bound.
No kernel may reach another device: no remote copies, remote signals or barrier semaphores. Data moves between devices by JAX's collectives and lax.ppermute only.
A program may use at most 192 MiB of HBM per device.

v0:
```python
import jax
import jax.numpy as jnp
from jax import lax
from jax.sharding import Mesh
from jax.sharding import PartitionSpec as P

W = 4096
K = 8
NSHIFT = 2
SHIFT_BINS = 16
WIN = 16
CAP = 128
BLK = ("blk_0", "blk_1", "blk_2")
BLK_REP = ("blk_0", "blk_1", "blk_2", "rep")
ZRING = ("blk_1", "rep")


def ring_index(z, core):
    return z // 2 * 4 + z % 2 * 2 + core


UP = [(ring_index(z, 0), ring_index((z + 1) % 4, 0)) for z in range(4)] + [
    (ring_index(z, 1), ring_index((z + 3) % 4, 1)) for z in range(4)
]
CROSS = [(ring_index(z, 1), ring_index((z + 1) % 4, 0)) for z in range(4)] + [
    (ring_index(z, 0), ring_index((z + 3) % 4, 1)) for z in range(4)
]
SIBLING = [(ring_index(z, c), ring_index(z, 1 - c)) for z in range(4) for c in range(2)]


def inverse(perm):
    return [(b, a) for a, b in perm]


def unit_rows(raw):
    values = jnp.sqrt(raw.astype(jnp.float32))
    total = jnp.sum(values * values, axis=-1, keepdims=True)
    return (values * lax.rsqrt(total + 1e-06)).astype(jnp.bfloat16)


def lower_bins(rows, amount):
    tail = jnp.zeros(rows.shape[:-1] + (amount,), rows.dtype)
    return jnp.concatenate([rows[..., amount:], tail], axis=-1)


def slot_index(role, roles, capacity):
    labels = jnp.arange(roles, dtype=jnp.int32)
    onehot = (role[:, None] == labels[None, :]).astype(jnp.int32)
    before = jnp.cumsum(onehot, axis=0) - onehot
    place = jnp.sum(before * onehot, axis=1)
    return role * capacity + place


def top_rows(scores):
    height = scores.shape[0]
    position = lax.broadcasted_iota(jnp.int32, scores.shape, 0)
    picked = []
    for step in range(K):
        top = jnp.max(scores, axis=0)
        first = jnp.min(jnp.where(scores == top[None, :], position, height), axis=0)
        picked.append(top)
        scores = jnp.where(position == first[None, :], -3e38, scores)
    return jnp.stack(picked, axis=1)


def route(blocks, perms):
    return [blocks[0]] + [lax.ppermute(b, ZRING, p) for b, p in zip(blocks[1:], perms)]


def on_device(queries, query_group, query_bin, query_shift, library, library_bin):
    lib_rows = library.shape[1]
    z_lo = lax.axis_index("rep") // 2
    core = lax.axis_index("rep") % 2
    roles = 4
    slots = roles * CAP
    unit_lib = unit_rows(library[0])
    bin_row = jnp.pad(library_bin.astype(jnp.bfloat16), ((0, 0), (0, W - lib_rows)))
    packed_lib = jnp.concatenate([unit_lib, bin_row], axis=0)
    half = lax.all_gather(packed_lib, "blk_1", axis=0, tiled=True)
    full = lax.all_gather(half, ("blk_0", "blk_2"), axis=0, tiled=True)
    stride = lib_rows + 1
    blocks_n = full.shape[0] // stride
    lib_bins = full.reshape(blocks_n, stride, W)[:, lib_rows, :stride].reshape(-1)
    lib_bins = lib_bins.astype(jnp.int32)
    valid = jnp.arange(full.shape[0], dtype=jnp.int32) % stride != lib_rows
    unit_q = unit_rows(queries)
    group = query_group[:, 0]
    role = (group // 2 != z_lo).astype(jnp.int32) * 2 + (group % 2 != core).astype(jnp.int32)
    slot = slot_index(role, roles, CAP)
    slot_ids = jnp.arange(slots, dtype=jnp.int32)
    placed = slot[:, None] == slot_ids[None, :]
    placed_int = placed.astype(jnp.int32)
    send_q = (
        lax.dot_general(
            placed.astype(jnp.bfloat16),
            unit_q,
            (((0,), (0,)), ((), ())),
            preferred_element_type=jnp.float32,
        )
        .astype(jnp.bfloat16)
        .reshape(roles, CAP, W)
    )
    send_bin = jnp.sum(placed_int * query_bin[:, None], axis=0).reshape(roles, CAP)
    send_shift = jnp.sum(placed_int * query_shift[:, None], axis=0).reshape(roles, CAP)
    send_meta = jnp.stack([send_bin, send_shift], axis=1)
    perms = (SIBLING, UP, CROSS)
    rows = jnp.concatenate(route([send_q[i] for i in range(roles)], perms), axis=0)
    meta = jnp.stack(route([send_meta[i] for i in range(roles)], perms), axis=0)
    flat_bin = meta[:, 0].reshape(-1)
    flat_shift = meta[:, 1].reshape(-1)
    total = rows.shape[0]
    moved = jnp.zeros_like(rows)
    for s in range(1, NSHIFT + 1):
        moved = jnp.where((flat_shift == s)[:, None], lower_bins(rows, s * SHIFT_BINS), moved)
    both = jnp.concatenate([rows, moved], axis=0)
    prod = lax.dot_general(full, both, (((1,), (1,)), ((), ())), preferred_element_type=jnp.float32)
    near = (jnp.abs(lib_bins[:, None] - flat_bin[None, :]) <= WIN) & valid[:, None]
    scores = jnp.where(near, jnp.maximum(prod[:, :total], prod[:, total:]), 0.0)
    scores = jnp.where(valid[:, None], scores, -1.0)
    best = top_rows(scores).reshape(roles, CAP, K)
    home = route([best[i] for i in range(roles)], tuple((inverse(p) for p in perms)))
    home = jnp.concatenate(home, axis=0)
    return jnp.take(home, slot, axis=0)


def solution(mesh):
    split = Mesh(
        mesh.devices.reshape(4, 2, 4, mesh.shape["rep"]), ("blk_0", "blk_1", "blk_2", "rep")
    )
    in_specs = (
        P(BLK_REP, None),
        P(BLK_REP, None),
        P(BLK_REP),
        P(BLK_REP),
        P("rep", BLK, None),
        P("rep", BLK),
    )
    out_specs = P(BLK_REP, None)
    return jax.shard_map(
        on_device, mesh=split, in_specs=in_specs, out_specs=out_specs, check_vma=False
    )
```

profile of v0, /device:TPU:0, one launch (start us, length us, event | category | flops | bytes accessed | tf_op | source)
XLA Modules:
  0.0 165.7 jit_solution(16801492224332433308)
XLA Ops:
  6.5 1.4 fusion.15
  7.9 1.1 fusion.16
  9.1 0.7 convert_element_type.53
  9.7 12.3 %all-gather = bf16[2,33,4096]{2,1,0:T(8,128)(2,1)S(1)} all-gather(bf16[1,33,4096]{2,1,0:T(8,128)(2,1)S(1)} %fusion.18), channel_id=1, replica_groups=mesh['blk_0'=4,'blk_1'=2,'blk_2'=4,'rep'=4] {'blk_1'}, dimensions={0}, use_global_device_ids=true | all-gather | bytes 811008 | tf_op jit(solution)/shard_map/all_gather | solution.py:79
  22.1 0.9 reshape.119
  23.1 1.2 reduce-window.6
  24.8 1.4 multiply_reduce_fusion
  26.2 2.0 %convolution_convert_fusion = bf16[512,4096]{1,0:T(8,128)(2,1)S(1)} fusion(bf16[256,4096]{1,0:T(8,128)(2,1)S(1)} %copy-done, f32[256]{0:T(256)S(1)} %add_rsqrt_fusion, s32[256]{0:T(256)S(1)} %bitcast.72), kind=kOutput, calls=%fused_computation.1 | convolution fusion | flops 1079115776 | bytes 6293504 | tf_op jit(solution)/shard_map/dot_general | solution.py:94
  28.2 1.7 %fusion.39 = (bf16[128,4096]{1,0:T(8,128)(2,1)S(1)}, bf16[1024,4096]{1,0:T(8,128)(2,1)}, bf16[128,4096]{1,0:T(8,128)(2,1)S(1)}, bf16[128,4096]{1,0:T(8,128)(2,1)S(1)}, bf16[128,4096]{1,0:T(8,128)(2,1)S(1)}) fusion(bf16[512,4096]{1,0:T(8,128)(2,1)S(1)} %convolution_convert_fusion), kind=kLoop, calls=%fused_computation.106 | loop fusion | bytes 9437184 | tf_op jit(solution)/shard_map/slice | solution.py:107
  29.9 1.3 collective-permute-start.4
  31.2 2.3 %collective-permute-start.5 = (bf16[128,4096]{1,0:T(8,128)(2,1)S(1)}, bf16[128,4096]{1,0:T(8,128)(2,1)S(1)}, u32[]{:S(2)}, u32[]{:S(2)}) collective-permute-start(bf16[128,4096]{1,0:T(8,128)(2,1)S(1)} %get-tuple-element.14), channel_id=1, source_target_pairs={{1,2},{3,16},{17,18},{19,0},{0,19},{2,1},{16,3},{18,17},{5,6},{7,2... | collective-permute-start | bytes 3145736 | tf_op jit(solution)/shard_map/ppermute | solution.py:67
  33.6 0.2 select_reduce_fusion.9
  33.9 1.7 %collective-permute-start.1 = (s32[2,128]{1,0:T(2,128)S(1)}, s32[2,128]{1,0:T(2,128)S(1)}, u32[]{:S(2)}, u32[]{:S(2)}) collective-permute-start(s32[2,128]{1,0:T(2,128)S(1)} %get-tuple-element.26), channel_id=1, source_target_pairs={{0,2},{2,16},{16,18},{18,0},{1,19},{3,1},{17,3},{19,17},{4,6},{6,2... | collective-permute-start | bytes 3080 | tf_op jit(solution)/shard_map/ppermute | solution.py:67
  35.5 0.2 collective-permute-start.2
  35.7 21.2 %collective-permute-done.1 = s32[2,128]{1,0:T(2,128)S(1)} collective-permute-done((s32[2,128]{1,0:T(2,128)S(1)}, s32[2,128]{1,0:T(2,128)S(1)}, u32[]{:S(2)}, u32[]{:S(2)}) %collective-permute-start.1) | collective-permute-done | bytes 1056 | tf_op jit(solution)/shard_map/ppermute | solution.py:67
  56.9 0.5 collective-permute-done.2
  57.5 0.5 pad_maximum_fusion
  58.0 3.2 %slice.108 = bf16[512,4064]{1,0:T(8,128)(2,1)S(1)} slice(bf16[512,4096]{1,0:T(8,128)(2,1)S(1)} %pad_maximum_fusion), slice={[0:512], [32:4096]} | slice | bytes 8323072 | tf_op jit(solution)/shard_map/slice | solution.py:43
  61.2 3.2 %slice.109 = bf16[512,4080]{1,0:T(8,128)(2,1)S(1)} slice(bf16[512,4096]{1,0:T(8,128)(2,1)S(1)} %pad_maximum_fusion), slice={[0:512], [16:4096]} | slice | bytes 8355840 | tf_op jit(solution)/shard_map/slice | solution.py:43
  64.4 1.1 constant_dynamic-update-slice_fusion.2
  65.5 1.1 constant_dynamic-update-slice_fusion.1
  66.5 1.1 constant_dynamic-update-slice_fusion
  67.6 4.1 %select_dynamic-update-slice_fusion = bf16[1024,4096]{1,0:T(8,128)(2,1)} fusion(bf16[1024,4096]{1,0:T(8,128)(2,1)} %constant_dynamic-update-slice_fusion, bf16[512,4080]{1,0:T(8,128)(2,1)S(1)} %slice.109, bf16[512,4064]{1,0:T(8,128)(2,1)S(1)} %slice.108, pred[512]{0:T(512)(128)(4,1)S(1)} %get-tuple-element.22, pred[512]{0:T(512)(128)(4,1)S(1)} %get-tuple-element.21), kind=kLoop, calls=%fused_computation.3 | loop fusion | flops 4194304 | bytes 12534784 | tf_op jit(solution)/shard_map/concatenate | solution.py:115
  71.8 28.8 %all-gather.4.cloned.1.call-done = bf16[16,66,4096]{2,1,0:T(8,128)(2,1)} async-done(((bf16[1,66,4096]{2,1,0:T(8,128)(2,1)}), bf16[16,66,4096]{2,1,0:T(8,128)(2,1)}) %all-gather.4.cloned.1.call-update) | async-done | bytes 8650768 | tf_op jit(solution)/shard_map/all_gather | solution.py:80
  100.6 13.2 %reshape.107 = bf16[32,33,4096]{2,1,0:T(8,128)(2,1)} reshape(bf16[16,66,4096]{2,1,0:T(8,128)(2,1)} %all-gather.4.cloned.1.call-done) | data formatting | bytes 17301504 | tf_op jit(solution)/shard_map/reshape | solution.py:83
  113.7 0.9 fusion.21
  114.7 8.2 %reshape.120 = bf16[1056,4096]{1,0:T(8,128)(2,1)} reshape(bf16[16,66,4096]{2,1,0:T(8,128)(2,1)} %all-gather.4.cloned.1.call-done) | data formatting | bytes 17301504
  122.9 13.0 %fusion.41 = f32[1056,1024]{1,0:T(8,128)S(1)} fusion(bf16[1056,4096]{1,0:T(8,128)(2,1)} %reshape.120, bf16[1024,4096]{1,0:T(8,128)(2,1)} %select_dynamic-update-slice_fusion), kind=kOutput, calls=%fused_computation.108 | convolution fusion | flops 8858370048 | bytes 21364736 | tf_op jit(solution)/shard_map/dot_general | solution.py:116
  135.9 1.4 fusion.37
  137.3 0.4 select_reduce_fusion.7
  137.7 0.4 fusion.13
  138.0 0.5 select_reduce_fusion.6
  138.6 0.5 fusion.12
  139.1 0.8 select_reduce_fusion.5
  139.8 0.7 fusion.36
  140.5 0.9 select_reduce_fusion.4
  141.4 0.8 fusion.11
  142.3 1.1 select_reduce_fusion.3
  143.4 1.0 fusion.20
  144.5 1.3 select_reduce_fusion.2
  145.7 1.2 fusion.10
  147.0 1.5 select_reduce_fusion.1
  148.4 1.4 select_reduce_fusion
  149.9 3.0 %collective-permute-start.7 = (f32[128,8]{0,1:T(8,128)S(1)}, f32[128,8]{0,1:T(8,128)S(1)}, u32[]{:S(2)}, u32[]{:S(2)}) collective-permute-start(f32[128,8]{0,1:T(8,128)S(1)} %get-tuple-element.19), channel_id=1, source_target_pairs={{2,0},{16,2},{18,16},{0,18},{19,1},{1,3},{3,17},{17,19},{6,4},{20,... | collective-permute-start | bytes 12296 | tf_op jit(solution)/shard_map/ppermute | solution.py:67
  153.0 1.3 collective-permute-done.7
  154.3 2.9 %collective-permute-done.8 = f32[128,8]{0,1:T(8,128)S(1)} collective-permute-done((f32[128,8]{0,1:T(8,128)S(1)}, f32[128,8]{0,1:T(8,128)S(1)}, u32[]{:S(2)}, u32[]{:S(2)}) %collective-permute-start.8) | collective-permute-done | bytes 4128 | tf_op jit(solution)/shard_map/ppermute | solution.py:67
  157.3 0.7 gather_fusion
  158.2 0.7 copy.37
  (44 shorter events, 1.2 us)
Async XLA Ops:
  6.5 16.5 %copy-start.1 = (s32[256,1]{0,1:T(1,128)S(1)}, s32[256,1]{0,1:T(1,128)}, u32[]{:S(2)}) copy-start(s32[256,1]{0,1:T(1,128)} %param.7) | copy-start | bytes 3076
  6.5 18.2 %copy-start = (bf16[256,4096]{1,0:T(8,128)(2,1)S(1)}, bf16[256,4096]{1,0:T(8,128)(2,1)}, u32[]{:S(2)}) copy-start(bf16[256,4096]{1,0:T(8,128)(2,1)} %param.6) | copy-start | bytes 6291460
  6.5 94.0 %all-gather.4.cloned.1.call-start = ((), (), s32[]{:S(2)}) async-start(), calls=%async_computation | async-start | bytes 10027008 | tf_op jit(solution)/shard_map/all_gather | solution.py:80
  28.2 5.4 %copy-start.2 = (s32[256]{0:T(256)S(1)}, s32[256]{0:T(256)}, u32[]{:S(2)}) copy-start(s32[256]{0:T(256)} %param.8) | copy-start | bytes 3076
  28.2 5.3 %copy-start.3 = (s32[256]{0:T(256)S(1)}, s32[256]{0:T(256)}, u32[]{:S(2)}) copy-start(s32[256]{0:T(256)} %param.9) | copy-start | bytes 3076
  29.9 27.5 %collective-permute-start.3 = (bf16[128,4096]{1,0:T(8,128)(2,1)S(1)}, bf16[128,4096]{1,0:T(8,128)(2,1)S(1)}, u32[]{:S(2)}, u32[]{:S(2)}) collective-permute-start(bf16[128,4096]{1,0:T(8,128)(2,1)S(1)} %get-tuple-element.16), channel_id=1, source_target_pairs={{0,1},{1,0},{2,3},{3,2},{16,17},{17,16},{18,19},{19,18},{4,5},{5,4... | collective-permute-start | bytes 3145736 | tf_op jit(solution)/shard_map/ppermute | solution.py:67
  29.9 27.5 %collective-permute-start.4 = (bf16[128,4096]{1,0:T(8,128)(2,1)S(1)}, bf16[128,4096]{1,0:T(8,128)(2,1)S(1)}, u32[]{:S(2)}, u32[]{:S(2)}) collective-permute-start(bf16[128,4096]{1,0:T(8,128)(2,1)S(1)} %get-tuple-element.15), channel_id=1, source_target_pairs={{0,2},{2,16},{16,18},{18,0},{1,19},{3,1},{17,3},{19,17},{4,6},{6,2... | collective-permute-start | bytes 3145736 | tf_op jit(solution)/shard_map/ppermute | solution.py:67
  31.2 26.2 %collective-permute-start.5 = (bf16[128,4096]{1,0:T(8,128)(2,1)S(1)}, bf16[128,4096]{1,0:T(8,128)(2,1)S(1)}, u32[]{:S(2)}, u32[]{:S(2)}) collective-permute-start(bf16[128,4096]{1,0:T(8,128)(2,1)S(1)} %get-tuple-element.14), channel_id=1, source_target_pairs={{1,2},{3,16},{17,18},{19,0},{0,19},{2,1},{16,3},{18,17},{5,6},{7,2... | collective-permute-start | bytes 3145736 | tf_op jit(solution)/shard_map/ppermute | solution.py:67
  33.8 1.8 %collective-permute-start = (s32[2,128]{1,0:T(2,128)S(1)}, s32[2,128]{1,0:T(2,128)S(1)}, u32[]{:S(2)}, u32[]{:S(2)}) collective-permute-start(s32[2,128]{1,0:T(2,128)S(1)} %get-tuple-element.24), channel_id=1, source_target_pairs={{0,1},{1,0},{2,3},{3,2},{16,17},{17,16},{18,19},{19,18},{4,5},{5,4... | collective-permute-start | bytes 3080 | tf_op jit(solution)/shard_map/ppermute | solution.py:67
  33.9 23.0 %collective-permute-start.1 = (s32[2,128]{1,0:T(2,128)S(1)}, s32[2,128]{1,0:T(2,128)S(1)}, u32[]{:S(2)}, u32[]{:S(2)}) collective-permute-start(s32[2,128]{1,0:T(2,128)S(1)} %get-tuple-element.26), channel_id=1, source_target_pairs={{0,2},{2,16},{16,18},{18,0},{1,19},{3,1},{17,3},{19,17},{4,6},{6,2... | collective-permute-start | bytes 3080 | tf_op jit(solution)/shard_map/ppermute | solution.py:67
  35.5 21.8 %collective-permute-start.2 = (s32[2,128]{1,0:T(2,128)S(1)}, s32[2,128]{1,0:T(2,128)S(1)}, u32[]{:S(2)}, u32[]{:S(2)}) collective-permute-start(s32[2,128]{1,0:T(2,128)S(1)} %get-tuple-element.25), channel_id=1, source_target_pairs={{1,2},{3,16},{17,18},{19,0},{0,19},{2,1},{16,3},{18,17},{5,6},{7,2... | collective-permute-start | bytes 3080 | tf_op jit(solution)/shard_map/ppermute | solution.py:67
  149.8 3.2 %collective-permute-start.6 = (f32[128,8]{0,1:T(8,128)S(1)}, f32[128,8]{0,1:T(8,128)S(1)}, u32[]{:S(2)}, u32[]{:S(2)}) collective-permute-start(f32[128,8]{0,1:T(8,128)S(1)} %get-tuple-element.20), channel_id=1, source_target_pairs={{1,0},{0,1},{3,2},{2,3},{17,16},{16,17},{19,18},{18,19},{5,4},{4,5... | collective-permute-start | bytes 12296 | tf_op jit(solution)/shard_map/ppermute | solution.py:67
  149.9 4.3 %collective-permute-start.7 = (f32[128,8]{0,1:T(8,128)S(1)}, f32[128,8]{0,1:T(8,128)S(1)}, u32[]{:S(2)}, u32[]{:S(2)}) collective-permute-start(f32[128,8]{0,1:T(8,128)S(1)} %get-tuple-element.19), channel_id=1, source_target_pairs={{2,0},{16,2},{18,16},{0,18},{19,1},{1,3},{3,17},{17,19},{6,4},{20,... | collective-permute-start | bytes 12296 | tf_op jit(solution)/shard_map/ppermute | solution.py:67
  153.0 4.2 %collective-permute-start.8 = (f32[128,8]{0,1:T(8,128)S(1)}, f32[128,8]{0,1:T(8,128)S(1)}, u32[]{:S(2)}, u32[]{:S(2)}) collective-permute-start(f32[128,8]{0,1:T(8,128)S(1)} %get-tuple-element.18), channel_id=1, source_target_pairs={{2,1},{16,3},{18,17},{0,19},{19,0},{1,2},{3,16},{17,18},{6,5},{20,... | collective-permute-start | bytes 12296 | tf_op jit(solution)/shard_map/ppermute | solution.py:67
Sparse Core Ops, SparseCore 0:
  23.2 77.3 all-gather.3
where the time goes:
time: 166 us
  waiting for transfers between devices  54.7 us (33%)
  local copies, waits for them, and re-layouts  35.5 us (21%)
  other arithmetic  25.8 us (16%)
  matrix products  15 us (9%)
  between operations  13.6 us (8%)
  blocking collectives  12.3 us (7%)
  starting transfers between devices  8.72 us (5%)
    all_gather x1, waiting for transfers between devices, on_device(): full = lax.all_gather(half, ('blk_0', 'blk_2'), axis=0, tiled=True)  28.8 us
    ppermute x9, waiting for transfers between devices, route(): lax.ppermute(b, ZRING, p)  25.9 us
    reshape x1, local copies, waits for them, and re-layouts, on_device(): full.reshape(blocks_n, stride, W)[:, lib_rows, :stride].reshape(-1)  13.2 us
    dot_general x1, matrix products, on_device(): lax.dot_general(full, both, (((1,), (1,)), ((), ())), preferred_element_t...  13 us
    all_gather x1, blocking collectives, on_device(): half = lax.all_gather(packed_lib, 'blk_1', axis=0, tiled=True)  12.3 us
    unnamed x13, local copies, waits for them, and re-layouts  12.3 us
    ppermute x9, starting transfers between devices, route(): lax.ppermute(b, ZRING, p)  8.72 us
    reduce_max x8, other arithmetic, top_rows(): top = jnp.max(scores, axis=0)  7.39 us
  transfers between devices with their start and end apart: 10, of which 5 were waited for; matrix products, arithmetic and copies ran while one was open for 13% of the time, Pallas kernels for 0%

commit v1 on v0

--- a/solution.py
+++ b/solution.py
@@ -77,7 +77,10 @@
     bin_row = jnp.pad(library_bin.astype(jnp.bfloat16), ((0, 0), (0, W - lib_rows)))
     packed_lib = jnp.concatenate([unit_lib, bin_row], axis=0)
     half = lax.all_gather(packed_lib, "blk_1", axis=0, tiled=True)
-    full = lax.all_gather(half, ("blk_0", "blk_2"), axis=0, tiled=True)
+    devices = lax.axis_size(("blk_0", "blk_2"))
+    pieces = jnp.stack([half for _ in range(devices)])
+    pieces = lax.all_to_all(pieces, ("blk_0", "blk_2"), split_axis=0, concat_axis=0)
+    full = jnp.concatenate(pieces, axis=0)
     stride = lib_rows + 1
     blocks_n = full.shape[0] // stride
     lib_bins = full.reshape(blocks_n, stride, W)[:, lib_rows, :stride].reshape(-1)

time: 166 us -> 248 us (1.49); the launches traced: 166 us -> 245 us
  waiting for transfers between devices: 54.7 us -> 136 us
  between operations: 13.6 us -> 0.27 us
  starting transfers between devices: 8.72 us -> 16 us
  local copies, waits for them, and re-layouts: 35.5 us -> 39.5 us
    all_to_all x0 -> x1, waiting for transfers between devices: none -> 113 us  [on_device(): lax.all_to_all(pieces, ('blk_0', 'blk_2'), split_axis=0, concat_axis=0)]
    all_gather x1 -> x0, waiting for transfers between devices: 28.8 us -> none  [on_device(): full = lax.all_gather(half, ('blk_0', 'blk_2'), axis=0, tiled=True)]
    another operation x2 -> x4, local copies, waits for them, and re-layouts: 0.1 us -> 18.1 us  [the longest x1 13.2 us: on_device(): full.reshape(blocks_n, stride, W)[:, lib_rows, :stride].reshape(-1)]
    unnamed x13 -> x12, local copies, waits for them, and re-layouts: 12.3 us -> 3.37 us
    all_to_all x0 -> x1, starting transfers between devices: none -> 7.21 us  [on_device(): lax.all_to_all(pieces, ('blk_0', 'blk_2'), split_axis=0, concat_axis=0)]
    reshape x1, local copies, waits for them, and re-layouts: 13.2 us -> 8.16 us  [on_device(): full = jnp.concatenate(pieces, axis=0)]
    ppermute x9, waiting for transfers between devices: 25.9 us -> 23 us  [route(): lax.ppermute(b, ZRING, p)]
  transfers between devices with their start and end apart: 10 -> 10, of which waited for: 5 -> 5; matrix products, arithmetic and copies ran while one was open for 13% -> 9% of each run, Pallas kernels for 0% -> 0%
where the time goes in v1:
time: 248 us; the launch traced here: 245 us
  waiting for transfers between devices  136 us (55%)
  local copies, waits for them, and re-layouts  39.5 us (16%)
  other arithmetic  25.7 us (10%)
  starting transfers between devices  16 us (6%)
  matrix products  14.9 us (6%)
  blocking collectives  12.3 us (5%)
    all_to_all x1, waiting for transfers between devices, on_device(): lax.all_to_all(pieces, ('blk_0', 'blk_2'), split_axis=0, concat_axis=0)  113 us
    ppermute x9, waiting for transfers between devices, route(): lax.ppermute(b, ZRING, p)  23 us
    another operation x1, local copies, waits for them, and re-layouts, on_device(): full.reshape(blocks_n, stride, W)[:, lib_rows, :stride].reshape(-1)  13.2 us
    dot_general x1, matrix products, on_device(): lax.dot_general(full, both, (((1,), (1,)), ((), ())), preferred_element_t...  13 us
    all_gather x1, blocking collectives, on_device(): half = lax.all_gather(packed_lib, 'blk_1', axis=0, tiled=True)  12.3 us
    ppermute x9, starting transfers between devices, route(): lax.ppermute(b, ZRING, p)  8.76 us
    reshape x1, local copies, waits for them, and re-layouts, on_device(): full = jnp.concatenate(pieces, axis=0)  8.16 us
    reduce_max x8, other arithmetic, top_rows(): top = jnp.max(scores, axis=0)  7.39 us
  transfers between devices with their start and end apart: 10, of which 5 were waited for; matrix products, arithmetic and copies ran while one was open for 9% of the time, Pallas kernels for 0%

profile of v1, /device:TPU:0, one launch (start us, length us, event | category | flops | bytes accessed | tf_op | source)
XLA Modules:
  0.0 245.0 jit_solution(3776104924431081186)
XLA Ops:
  0.0 1.2 fusion.15
  1.2 1.1 fusion.16
  2.4 0.7 convert_element_type.53
  3.1 12.3 %all-gather = bf16[2,33,4096]{2,1,0:T(8,128)(2,1)S(1)} all-gather(bf16[1,33,4096]{2,1,0:T(8,128)(2,1)S(1)} %fusion.18), channel_id=1, replica_groups=mesh['blk_0'=4,'blk_1'=2,'blk_2'=4,'rep'=4] {'blk_1'}, dimensions={0}, use_global_device_ids=true | all-gather | bytes 811008 | tf_op jit(solution)/shard_map/all_gather | solution.py:79
  15.5 4.8 %stack.30 = bf16[16,66,4096]{2,1,0:T(8,128)(2,1)} broadcast(bf16[66,4096]{1,0:T(8,128)(2,1)S(1)} %reshape.120), dimensions={1,2} | broadcast | bytes 9191424 | tf_op jit(solution)/shard_map/stack | solution.py:81
  20.3 7.2 %all-to-all-start = ((bf16[16,66,4096]{2,1,0:T(8,128)(2,1)}), bf16[16,66,4096]{2,1,0:T(8,128)(2,1)}, u32[]{:S(2)}, u32[]{:S(2)}) async-start(bf16[16,66,4096]{2,1,0:T(8,128)(2,1)} %stack.30), calls=%async_computation | async-start | bytes 18874368 | tf_op jit(solution)/shard_map/all_to_all | solution.py:82
  27.6 1.2 reduce-window.6
  29.3 1.4 multiply_reduce_fusion
  30.7 2.0 convolution_convert_fusion
  32.7 1.7 fusion.39
  34.4 1.3 collective-permute-start.4
  35.7 2.4 collective-permute-start.5
  38.1 0.2 select_reduce_fusion.9
  38.4 1.7 collective-permute-start.1
  40.3 21.2 %collective-permute-done.1 = s32[2,128]{1,0:T(2,128)S(1)} collective-permute-done((s32[2,128]{1,0:T(2,128)S(1)}, s32[2,128]{1,0:T(2,128)S(1)}, u32[]{:S(2)}, u32[]{:S(2)}) %collective-permute-start.1) | collective-permute-done | bytes 1056 | tf_op jit(solution)/shard_map/ppermute | solution.py:67
  61.4 0.5 collective-permute-done.2
  62.0 0.5 pad_maximum_fusion
  62.5 3.2 %slice.108 = bf16[512,4064]{1,0:T(8,128)(2,1)S(1)} slice(bf16[512,4096]{1,0:T(8,128)(2,1)S(1)} %pad_maximum_fusion), slice={[0:512], [32:4096]} | slice | bytes 8323072 | tf_op jit(solution)/shard_map/slice | solution.py:43
  65.7 3.2 %slice.109 = bf16[512,4080]{1,0:T(8,128)(2,1)S(1)} slice(bf16[512,4096]{1,0:T(8,128)(2,1)S(1)} %pad_maximum_fusion), slice={[0:512], [16:4096]} | slice | bytes 8355840 | tf_op jit(solution)/shard_map/slice | solution.py:43
  68.9 1.1 constant_dynamic-update-slice_fusion.2
  70.0 1.1 constant_dynamic-update-slice_fusion.1
  71.1 1.1 constant_dynamic-update-slice_fusion
  72.2 4.1 %select_dynamic-update-slice_fusion = bf16[1024,4096]{1,0:T(8,128)(2,1)} fusion(bf16[1024,4096]{1,0:T(8,128)(2,1)} %constant_dynamic-update-slice_fusion, bf16[512,4080]{1,0:T(8,128)(2,1)S(1)} %slice.109, bf16[512,4064]{1,0:T(8,128)(2,1)S(1)} %slice.108, pred[512]{0:T(512)(128)(4,1)S(1)} %get-tuple-element.22, pred[512]{0:T(512)(128)(4,1)S(1)} %get-tuple-element.21), kind=kLoop, calls=%fused_computation.3 | loop fusion | flops 4194304 | bytes 12534784 | tf_op jit(solution)/shard_map/concatenate | solution.py:118
  76.3 113.3 %all-to-all-done = bf16[16,66,4096]{2,1,0:T(8,128)(2,1)} async-done(((bf16[16,66,4096]{2,1,0:T(8,128)(2,1)}), bf16[16,66,4096]{2,1,0:T(8,128)(2,1)}, u32[]{:S(2)}, u32[]{:S(2)}) %all-to-all-start) | async-done | bytes 8650784 | tf_op jit(solution)/shard_map/all_to_all | solution.py:82
  189.6 13.2 %reshape_reshape.3 = bf16[32,33,4096]{2,1,0:T(8,128)(2,1)} reshape(bf16[16,66,4096]{2,1,0:T(8,128)(2,1)} %all-to-all-done) | data formatting | bytes 17301504 | tf_op jit(solution)/shard_map/reshape;reshape | solution.py:86
  202.7 0.9 fusion.21
  203.7 8.2 %reshape.109 = bf16[1056,4096]{1,0:T(8,128)(2,1)} reshape(bf16[16,66,4096]{2,1,0:T(8,128)(2,1)} %all-to-all-done) | data formatting | bytes 17301504 | tf_op jit(solution)/shard_map/reshape | solution.py:83
  211.9 13.0 %fusion.41 = f32[1056,1024]{1,0:T(8,128)S(1)} fusion(bf16[1056,4096]{1,0:T(8,128)(2,1)} %reshape.109, bf16[1024,4096]{1,0:T(8,128)(2,1)} %select_dynamic-update-slice_fusion), kind=kOutput, calls=%fused_computation.108 | convolution fusion | flops 8858370048 | bytes 21364736 | tf_op jit(solution)/shard_map/dot_general | solution.py:119
  224.9 1.4 fusion.37
  226.3 0.4 select_reduce_fusion.7
  226.7 0.4 fusion.13
  227.1 0.5 select_reduce_fusion.6
  227.6 0.5 fusion.12
  228.1 0.8 select_reduce_fusion.5
  228.9 0.7 fusion.36
  229.5 0.9 select_reduce_fusion.4
  230.5 0.8 fusion.11
  231.3 1.1 select_reduce_fusion.3
  232.4 1.0 fusion.20
  233.5 1.3 select_reduce_fusion.2
  234.7 1.2 fusion.10
  236.0 1.5 select_reduce_fusion.1
  237.4 1.4 select_reduce_fusion
  239.0 3.0 %collective-permute-start.8 = (f32[128,8]{0,1:T(8,128)S(1)}, f32[128,8]{0,1:T(8,128)S(1)}, u32[]{:S(2)}, u32[]{:S(2)}) collective-permute-start(f32[128,8]{0,1:T(8,128)S(1)} %get-tuple-element.18), channel_id=1, source_target_pairs={{2,1},{16,3},{18,17},{0,19},{19,0},{1,2},{3,16},{17,18},{6,5},{20,... | collective-permute-start | bytes 12296 | tf_op jit(solution)/shard_map/ppermute | solution.py:67
  242.0 0.6 collective-permute-done.7
  242.6 0.7 collective-permute-done.8
  243.5 0.7 gather_fusion
  244.3 0.7 copy.37
  (44 shorter events, 1.5 us)
Async XLA Ops:
  20.3 7.2 %copy-start.1 = (s32[256,1]{0,1:T(1,128)S(1)}, s32[256,1]{0,1:T(1,128)}, u32[]{:S(2)}) copy-start(s32[256,1]{0,1:T(1,128)} %param.7) | copy-start | bytes 3076
  20.3 8.9 %copy-start = (bf16[256,4096]{1,0:T(8,128)(2,1)S(1)}, bf16[256,4096]{1,0:T(8,128)(2,1)}, u32[]{:S(2)}) copy-start(bf16[256,4096]{1,0:T(8,128)(2,1)} %param.6) | copy-start | bytes 6291460
  20.3 169.2 %all-to-all-start = ((bf16[16,66,4096]{2,1,0:T(8,128)(2,1)}), bf16[16,66,4096]{2,1,0:T(8,128)(2,1)}, u32[]{:S(2)}, u32[]{:S(2)}) async-start(bf16[16,66,4096]{2,1,0:T(8,128)(2,1)} %stack.30), calls=%async_computation | async-start | bytes 18874368 | tf_op jit(solution)/shard_map/all_to_all | solution.py:82
  32.7 5.4 %copy-start.2 = (s32[256]{0:T(256)S(1)}, s32[256]{0:T(256)}, u32[]{:S(2)}) copy-start(s32[256]{0:T(256)} %param.8) | copy-start | bytes 3076
  32.7 5.4 %copy-start.3 = (s32[256]{0:T(256)S(1)}, s32[256]{0:T(256)}, u32[]{:S(2)}) copy-start(s32[256]{0:T(256)} %param.9) | copy-start | bytes 3076
  34.4 27.5 %collective-permute-start.3 = (bf16[128,4096]{1,0:T(8,128)(2,1)S(1)}, bf16[128,4096]{1,0:T(8,128)(2,1)S(1)}, u32[]{:S(2)}, u32[]{:S(2)}) collective-permute-start(bf16[128,4096]{1,0:T(8,128)(2,1)S(1)} %get-tuple-element.16), channel_id=1, source_target_pairs={{0,1},{1,0},{2,3},{3,2},{16,17},{17,16},{18,19},{19,18},{4,5},{5,4... | collective-permute-start | bytes 3145736 | tf_op jit(solution)/shard_map/ppermute | solution.py:67
  34.4 27.6 %collective-permute-start.4 = (bf16[128,4096]{1,0:T(8,128)(2,1)S(1)}, bf16[128,4096]{1,0:T(8,128)(2,1)S(1)}, u32[]{:S(2)}, u32[]{:S(2)}) collective-permute-start(bf16[128,4096]{1,0:T(8,128)(2,1)S(1)} %get-tuple-element.15), channel_id=1, source_target_pairs={{0,2},{2,16},{16,18},{18,0},{1,19},{3,1},{17,3},{19,17},{4,6},{6,2... | collective-permute-start | bytes 3145736 | tf_op jit(solution)/shard_map/ppermute | solution.py:67
  35.7 26.2 %collective-permute-start.5 = (bf16[128,4096]{1,0:T(8,128)(2,1)S(1)}, bf16[128,4096]{1,0:T(8,128)(2,1)S(1)}, u32[]{:S(2)}, u32[]{:S(2)}) collective-permute-start(bf16[128,4096]{1,0:T(8,128)(2,1)S(1)} %get-tuple-element.14), channel_id=1, source_target_pairs={{1,2},{3,16},{17,18},{19,0},{0,19},{2,1},{16,3},{18,17},{5,6},{7,2... | collective-permute-start | bytes 3145736 | tf_op jit(solution)/shard_map/ppermute | solution.py:67
  38.3 1.8 collective-permute-start
  38.4 23.1 %collective-permute-start.1 = (s32[2,128]{1,0:T(2,128)S(1)}, s32[2,128]{1,0:T(2,128)S(1)}, u32[]{:S(2)}, u32[]{:S(2)}) collective-permute-start(s32[2,128]{1,0:T(2,128)S(1)} %get-tuple-element.26), channel_id=1, source_target_pairs={{0,2},{2,16},{16,18},{18,0},{1,19},{3,1},{17,3},{19,17},{4,6},{6,2... | collective-permute-start | bytes 3080 | tf_op jit(solution)/shard_map/ppermute | solution.py:67
  40.1 21.8 %collective-permute-start.2 = (s32[2,128]{1,0:T(2,128)S(1)}, s32[2,128]{1,0:T(2,128)S(1)}, u32[]{:S(2)}, u32[]{:S(2)}) collective-permute-start(s32[2,128]{1,0:T(2,128)S(1)} %get-tuple-element.25), channel_id=1, source_target_pairs={{1,2},{3,16},{17,18},{19,0},{0,19},{2,1},{16,3},{18,17},{5,6},{7,2... | collective-permute-start | bytes 3080 | tf_op jit(solution)/shard_map/ppermute | solution.py:67
  238.9 3.2 %collective-permute-start.6 = (f32[128,8]{0,1:T(8,128)S(1)}, f32[128,8]{0,1:T(8,128)S(1)}, u32[]{:S(2)}, u32[]{:S(2)}) collective-permute-start(f32[128,8]{0,1:T(8,128)S(1)} %get-tuple-element.20), channel_id=1, source_target_pairs={{1,0},{0,1},{3,2},{2,3},{17,16},{16,17},{19,18},{18,19},{5,4},{4,5... | collective-permute-start | bytes 12296 | tf_op jit(solution)/shard_map/ppermute | solution.py:67
  239.0 3.7 %collective-permute-start.7 = (f32[128,8]{0,1:T(8,128)S(1)}, f32[128,8]{0,1:T(8,128)S(1)}, u32[]{:S(2)}, u32[]{:S(2)}) collective-permute-start(f32[128,8]{0,1:T(8,128)S(1)} %get-tuple-element.19), channel_id=1, source_target_pairs={{2,0},{16,2},{18,16},{0,18},{19,1},{1,3},{3,17},{17,19},{6,4},{20,... | collective-permute-start | bytes 12296 | tf_op jit(solution)/shard_map/ppermute | solution.py:67
  239.0 4.3 %collective-permute-start.8 = (f32[128,8]{0,1:T(8,128)S(1)}, f32[128,8]{0,1:T(8,128)S(1)}, u32[]{:S(2)}, u32[]{:S(2)}) collective-permute-start(f32[128,8]{0,1:T(8,128)S(1)} %get-tuple-element.18), channel_id=1, source_target_pairs={{2,1},{16,3},{18,17},{0,19},{19,0},{1,2},{3,16},{17,18},{6,5},{20,... | collective-permute-start | bytes 12296 | tf_op jit(solution)/shard_map/ppermute | solution.py:67
